TPU v7x, 512 devices: a whole 4x4x16 slice. The times are simulated.
512 devices in a mesh: leaf: 8 (over y_hi, x), level: 64 (over y_lo, z, core).
Axes of the slice: x: 4, y: 4 (y_hi: 2, y_lo: 2; y = y_hi * 2 + y_lo), z: 16, core: 2. Of those that a mesh axis runs over, the one named last changes fastest.
Arguments:
- points: bfloat16 [524288, 64], P(('leaf', 'level')), may hold values from -1.6953125 to 1.6953125
- sketch_matrix: bfloat16 [524288, 64], P(('leaf', 'level')), may hold values from -6 to 6
- leaf_order: int32 [512, 1024], P(('leaf', 'level')), may hold values from 0 to 1023, each once within a row
Outputs:
- products: float32 [524288, 256], P(('leaf', 'level'))
- gram_out: float32 [512, 4, 64, 64], P(('leaf', 'level'))
Inputs may be any that keep to these rules, and one draw needn't show every extreme that they name: `leaf_order`: each row is a permutation of 0 to 1023.
All inputs are finite; a program needn't handle non-finite values.
Results may differ from a plain program's by a relative error of at most 0.0029.
Values may be sent and summed in bfloat16 or wider, within the bound.
No kernel may reach another device: no remote copies, remote signals or barrier semaphores. Data moves between devices by JAX's collectives and lax.ppermute only.
A program may use at most 64 MiB of HBM per device.

v0:
```python
import math

import jax
import jax.numpy as jnp
from jax import lax
from jax.sharding import Mesh, PartitionSpec as P


def swapped(value, axis, stride):
    return exchanged(value, axis, 2**stride)


def exchanged(value, axis, mask):
    pairs = [(source, source ^ mask) for source in range(lax.axis_size(axis))]
    return lax.ppermute(value, axis, pairs)


def squares_of(coords):
    return jnp.sum(jnp.square(coords.astype(jnp.float32)), axis=-1)


def raw_product(row_pts, row_sq, cols, dim):
    col_pts = cols[:, :dim]
    col_sketch = cols[:, dim:]
    col_sq = squares_of(col_pts)
    cross = lax.dot_general(
        row_pts, col_pts, (((1,), (1,)), ((), ())), preferred_element_type=jnp.float32
    )
    distance = row_sq[:, None] + col_sq[None, :] - 2.0 * cross
    kernel = jnp.exp((2.0 * dim - distance) * (2.0 / dim)).astype(jnp.bfloat16)
    return jnp.dot(kernel, col_sketch, preferred_element_type=jnp.float32)


def gram_of(product):
    return jnp.dot(
        product.T, product, precision=lax.Precision.HIGHEST, preferred_element_type=jnp.float32
    )


def device_body(points, sketch_matrix, leaf_order):
    dim = points.shape[1]
    rows_n = points.shape[0]
    picks = leaf_order[0][:, None] == jnp.arange(rows_n, dtype=leaf_order.dtype)[None, :]
    located = jnp.dot(
        picks.astype(points.dtype), points, preferred_element_type=jnp.float32
    ).astype(points.dtype)
    row_sq = squares_of(located)
    packed = jnp.concatenate([located, sketch_matrix], axis=1)
    leaf_bits = lax.axis_size("leaf").bit_length() - 1
    top = leaf_bits - 1
    y_rows = swapped(located, "leaf", top)
    y_sq = squares_of(y_rows)
    cluster = [packed]
    other_pieces = []
    results = []
    grams = []
    for tier_num in range(top):
        sibs = [
            exchanged(packed, "leaf", mask) for mask in range(1 << tier_num, 2 << tier_num)
        ]
        sib = jnp.concatenate(sibs) if len(sibs) > 1 else sibs[0]
        product = raw_product(located, row_sq, sib, dim) / math.sqrt(sib.shape[0])
        results.append(product)
        grams.append(gram_of(product))
        cluster.append(sib)
    cluster = jnp.concatenate(cluster)
    other_pieces = [swapped(cluster, "pair", 0)]
    partner_near = raw_product(y_rows, y_sq, cluster, dim)
    partner_far = None
    for piece in other_pieces:
        part = raw_product(y_rows, y_sq, piece, dim)
        partner_far = part if partner_far is None else partner_far + part
    back = swapped(jnp.concatenate([partner_near, partner_far], axis=1), "leaf", top)
    rank = partner_near.shape[1]
    product = back[:, :rank] / math.sqrt(cluster.shape[0])
    results.append(product)
    grams.append(gram_of(product))
    own_far = None
    far_rows = 0
    for piece in other_pieces:
        part = lax.optimization_barrier(raw_product(located, row_sq, piece, dim))
        own_far = part if own_far is None else own_far + part
        far_rows += piece.shape[0]
    product = (own_far + back[:, rank:]) / math.sqrt(2 * far_rows)
    results.append(product)
    grams.append(gram_of(product))
    low = 1 << top
    pair_sum = grams[1]
    quad_sum = [grams[2], grams[3]]
    for mask in range(1, low):
        if mask == 1:
            got = exchanged(jnp.stack(grams[1:]), "leaf", mask)
            pair_sum = pair_sum + got[0]
            got = got[1:]
        else:
            got = exchanged(jnp.stack(grams[2:]), "leaf", mask)
        quad_sum = [quad_sum[0] + got[0], quad_sum[1] + got[1]]
    last = quad_sum[1] + exchanged(quad_sum[1], "leaf", low)
    done = [grams[0], pair_sum, quad_sum[0], last]
    stacked = jnp.stack(done)
    divisors = jnp.asarray(
        [float((1 << tier_num) * rows_n) for tier_num in range(len(grams))], jnp.float32
    )
    stacked = stacked / divisors[:, None, None]
    return (jnp.concatenate(results, axis=1), stacked[None])


def solution(mesh):
    n_leaf = mesh.shape["leaf"]
    n_level = mesh.shape["level"]
    fine = Mesh(mesh.devices.reshape(n_leaf, n_level // 2, 2), ("leaf", "lvl", "pair"))
    axes = ("leaf", "lvl", "pair")
    in_specs = (P(axes, None), P(axes, None), P(axes, None))
    out_specs = (P(axes, None), P(axes, None, None, None))
    return jax.shard_map(
        device_body, mesh=fine, in_specs=in_specs, out_specs=out_specs, check_vma=False
    )
```

profile of v0, /device:TPU:16, one launch (start us, length us, event | category | flops | bytes accessed | tf_op | source)
XLA Modules:
  0.0 87.7 jit_solution(13154185881365871487)
XLA Ops:
  0.6 0.0 copy-start
  0.6 0.0 copy-start.1
  0.7 0.9 %copy-done = bf16[1024,64]{0,1:T(8,128)(2,1)S(1)} copy-done((bf16[1024,64]{0,1:T(8,128)(2,1)S(1)}, bf16[1024,64]{0,1:T(8,128)(2,1)}, u32[]{:S(2)}) %copy-start) | copy-done | bytes 131096
  1.5 1.7 %multiply_reduce_fusion.5 = (f32[1024]{0:T(1024)S(1)}, bf16[1024,64]{0,1:T(8,128)(2,1)S(1)}) fusion(bf16[1024,64]{0,1:T(8,128)(2,1)S(1)} %copy-done, s32[1024]{0:T(1024)} %bitcast.69), kind=kOutput, calls=%fused_computation.36 | convolution fusion | flops 135527424 | bytes 270336 | tf_op jit(solution)/shard_map/dot_general | solution.py:44
  3.3 0.0 copy-done.1
  3.3 4.9 %collective-permute-start.1 = (bf16[1024,128]{0,1:T(8,128)(2,1)S(1)}, bf16[1024,128]{0,1:T(8,128)(2,1)S(1)}, u32[]{:S(2)}, u32[]{:S(2)}) collective-permute-start(bf16[1024,128]{0,1:T(8,128)(2,1)S(1)} %pad_maximum_fusion.3), channel_id=1, source_target_pairs={{0,128},{64,192},{128,0},{192,64},{256,384},{320,448},{384,256},{4... | collective-permute-start | bytes 786440 | tf_op jit(solution)/shard_map/ppermute | solution.py:15
  8.2 4.6 %collective-permute-start.3 = (bf16[1024,64]{0,1:T(8,128)(2,1)S(1)}, bf16[1024,64]{0,1:T(8,128)(2,1)S(1)}, u32[]{:S(2)}, u32[]{:S(2)}) collective-permute-start(bf16[1024,64]{0,1:T(8,128)(2,1)S(1)} %get-tuple-element.10), channel_id=1, source_target_pairs={{0,256},{64,320},{128,384},{192,448},{256,0},{320,64},{384,128},{4... | collective-permute-start | bytes 393224 | tf_op jit(solution)/shard_map/ppermute | solution.py:15
  12.8 1.9 %collective-permute-start.2 = (bf16[1024,128]{0,1:T(8,128)(2,1)S(1)}, bf16[1024,128]{0,1:T(8,128)(2,1)S(1)}, u32[]{:S(2)}, u32[]{:S(2)}) collective-permute-start(bf16[1024,128]{0,1:T(8,128)(2,1)S(1)} %pad_maximum_fusion.3), channel_id=1, source_target_pairs={{0,192},{64,128},{128,64},{192,0},{256,448},{320,384},{384,320},{4... | collective-permute-start | bytes 786440 | tf_op jit(solution)/shard_map/ppermute | solution.py:15
  14.7 5.4 %collective-permute-start = (bf16[1024,128]{0,1:T(8,128)(2,1)S(1)}, bf16[1024,128]{0,1:T(8,128)(2,1)S(1)}, u32[]{:S(2)}, u32[]{:S(2)}) collective-permute-start(bf16[1024,128]{0,1:T(8,128)(2,1)S(1)} %pad_maximum_fusion.3), channel_id=1, source_target_pairs={{0,64},{64,0},{128,192},{192,128},{256,320},{320,256},{384,448},{4... | collective-permute-start | bytes 786440 | tf_op jit(solution)/shard_map/ppermute | solution.py:15
  20.1 0.0 collective-permute-done.3
  20.2 0.0 collective-permute-done.1
  20.2 2.1 %collective-permute-done.2 = bf16[1024,128]{0,1:T(8,128)(2,1)S(1)} collective-permute-done((bf16[1024,128]{0,1:T(8,128)(2,1)S(1)}, bf16[1024,128]{0,1:T(8,128)(2,1)S(1)}, u32[]{:S(2)}, u32[]{:S(2)}) %collective-permute-start.2) | collective-permute-done | bytes 262176 | tf_op jit(solution)/shard_map/ppermute | solution.py:15
  22.3 0.1 multiply_reduce_fusion.2
  22.4 2.1 %collective-permute-done = bf16[1024,128]{0,1:T(8,128)(2,1)S(1)} collective-permute-done((bf16[1024,128]{0,1:T(8,128)(2,1)S(1)}, bf16[1024,128]{0,1:T(8,128)(2,1)S(1)}, u32[]{:S(2)}, u32[]{:S(2)}) %collective-permute-start) | collective-permute-done | bytes 262176 | tf_op jit(solution)/shard_map/ppermute | solution.py:15
  24.5 0.1 pad_maximum_fusion
  24.5 1.9 %collective-permute-start.4 = (bf16[4096,128]{0,1:T(8,128)(2,1)S(1)}, bf16[4096,128]{0,1:T(8,128)(2,1)}, u32[]{:S(2)}, u32[]{:S(2)}) collective-permute-start(bf16[4096,128]{0,1:T(8,128)(2,1)S(1)} %pad_maximum_fusion), channel_id=1, source_target_pairs={{0,1},{1,0},{2,3},{3,2},{4,5},{5,4},{6,7},{7,6},{8,9},{9,8},{10,11... | collective-permute-start | bytes 3145736 | tf_op jit(solution)/shard_map/ppermute | solution.py:15
  26.5 3.2 %fusion.8 = f32[1024,64]{0,1:T(8,128)S(1)} fusion(bf16[1024,64]{0,1:T(8,128)(2,1)S(1)} %get-tuple-element.10, f32[2048]{0:T(1024)S(1)} %multiply_reduce_fusion.2, f32[1024]{0:T(1024)S(1)} %get-tuple-element.9, bf16[2048,128]{0,1:T(8,128)(2,1)S(1)} %constant_dynamic-update-slice_fusion), kind=kOutput, calls=%fused_computation.14 | convolution fusion | flops 549519360 | bytes 929792 | tf_op jit(solution)/shard_map/dot_general | solution.py:31
  29.7 1.7 %fusion.7 = f32[1024,64]{0,1:T(8,128)S(1)} fusion(bf16[1024,64]{0,1:T(8,128)(2,1)S(1)} %get-tuple-element.10, f32[1024]{0:T(1024)S(1)} %multiply_reduce_fusion.4, f32[1024]{0:T(1024)S(1)} %get-tuple-element.9, bf16[1024,128]{0,1:T(8,128)(2,1)S(1)} %collective-permute-done), kind=kOutput, calls=%fused_computation.13 | convolution fusion | flops 274792448 | bytes 663552 | tf_op jit(solution)/shard_map/dot_general | solution.py:31
  31.4 0.4 fusion.51
  31.7 0.1 multiply_reduce_fusion.1
  31.9 6.1 %fusion.2 = f32[1024,64]{0,1:T(8,128)S(1)} fusion(bf16[1024,64]{0,1:T(8,128)(2,1)S(1)} %collective-permute-done.3, f32[4096]{0:T(1024)S(1)} %multiply_reduce_fusion.1, f32[1024]{0:T(1024)S(1)} %multiply_reduce_fusion.3, bf16[4096,128]{0,1:T(8,128)(2,1)S(1)} %pad_maximum_fusion), kind=kOutput, calls=%fused_computation.8 | convolution fusion | flops 1098907648 | bytes 1462272 | tf_op jit(solution)/shard_map/dot_general | solution.py:31
  38.0 0.0 collective-permute-done.4
  38.0 1.2 %multiply_reduce_fusion = f32[4096]{0:T(1024)S(1)} fusion(bf16[4096,128]{0,1:T(8,128)(2,1)} %collective-permute-done.4), kind=kLoop, calls=%fused_computation.19 | loop fusion | flops 782336 | bytes 540672 | tf_op jit(solution)/shard_map/reduce_sum | solution.py:19
  39.2 7.4 %fusion.3 = f32[1024,64]{0,1:T(8,128)S(1)} fusion(bf16[1024,64]{0,1:T(8,128)(2,1)S(1)} %collective-permute-done.3, f32[4096]{0:T(1024)S(1)} %multiply_reduce_fusion, f32[1024]{0:T(1024)S(1)} %multiply_reduce_fusion.3, bf16[4096,128]{0,1:T(8,128)(2,1)} %collective-permute-done.4), kind=kOutput, calls=%fused_computation.9 | convolution fusion | flops 1098907648 | bytes 1462272 | tf_op jit(solution)/shard_map/dot_general | solution.py:31
  46.7 3.3 %collective-permute-start.5 = (f32[1024,128]{0,1:T(8,128)S(1)}, f32[1024,128]{0,1:T(8,128)S(1)}, u32[]{:S(2)}, u32[]{:S(2)}) collective-permute-start(f32[1024,128]{0,1:T(8,128)S(1)} %pad_maximum_fusion.2), channel_id=1, source_target_pairs={{0,256},{64,320},{128,384},{192,448},{256,0},{320,64},{384,128},{4... | collective-permute-start | bytes 1572872 | tf_op jit(solution)/shard_map/ppermute | solution.py:15
  49.9 7.3 %fusion.4 = f32[1024,64]{0,1:T(8,128)S(1)} fusion(bf16[1024,64]{0,1:T(8,128)(2,1)S(1)} %get-tuple-element.10, f32[1024]{0:T(1024)S(1)} %get-tuple-element.9, f32[4096]{0:T(1024)S(1)} %multiply_reduce_fusion, bf16[4096,128]{0,1:T(8,128)(2,1)} %collective-permute-done.4), kind=kOutput, calls=%fused_computation.10 | convolution fusion | flops 1098907648 | bytes 1462272 | tf_op jit(solution)/shard_map/dot_general | solution.py:31
  57.2 7.2 %collective-permute-done.5 = f32[1024,128]{0,1:T(8,128)S(1)} collective-permute-done((f32[1024,128]{0,1:T(8,128)S(1)}, f32[1024,128]{0,1:T(8,128)S(1)}, u32[]{:S(2)}, u32[]{:S(2)}) %collective-permute-start.5) | collective-permute-done | bytes 524320 | tf_op jit(solution)/shard_map/ppermute | solution.py:15
  64.4 0.1 slice_multiply_fusion
  64.4 0.4 fusion.52
  64.8 0.4 fusion.50
  65.2 3.7 %collective-permute-start.8 = (f32[2,64,64]{2,1,0:T(8,128)S(1)}, f32[2,64,64]{2,1,0:T(8,128)S(1)}, u32[]{:S(2)}, u32[]{:S(2)}) collective-permute-start(f32[2,64,64]{2,1,0:T(8,128)S(1)} %pad_maximum_fusion.5), channel_id=1, source_target_pairs={{0,192},{64,128},{128,64},{192,0},{256,448},{320,384},{384,320},{4... | collective-permute-start | bytes 98312 | tf_op jit(solution)/shard_map/ppermute | solution.py:15
  68.9 4.2 %collective-permute-start.7 = (f32[2,64,64]{2,1,0:T(8,128)S(1)}, f32[2,64,64]{2,1,0:T(8,128)S(1)}, u32[]{:S(2)}, u32[]{:S(2)}) collective-permute-start(f32[2,64,64]{2,1,0:T(8,128)S(1)} %pad_maximum_fusion.5), channel_id=1, source_target_pairs={{0,128},{64,192},{128,0},{192,64},{256,384},{320,448},{384,256},{4... | collective-permute-start | bytes 98312 | tf_op jit(solution)/shard_map/ppermute | solution.py:15
  73.1 1.9 %collective-permute-start.6 = (f32[3,64,64]{2,1,0:T(8,128)S(1)}, f32[3,64,64]{2,1,0:T(8,128)S(1)}, u32[]{:S(2)}, u32[]{:S(2)}) collective-permute-start(f32[3,64,64]{2,1,0:T(8,128)S(1)} %pad_maximum_fusion.4), channel_id=1, source_target_pairs={{0,64},{64,0},{128,192},{192,128},{256,320},{320,256},{384,448},{4... | collective-permute-start | bytes 147464 | tf_op jit(solution)/shard_map/ppermute | solution.py:15
  75.1 0.4 convolution_bitcast_fusion
  75.4 0.0 collective-permute-done.8
  75.4 1.1 %collective-permute-done.7 = f32[2,64,64]{2,1,0:T(8,128)S(1)} collective-permute-done((f32[2,64,64]{2,1,0:T(8,128)S(1)}, f32[2,64,64]{2,1,0:T(8,128)S(1)}, u32[]{:S(2)}, u32[]{:S(2)}) %collective-permute-start.7) | collective-permute-done | bytes 32800 | tf_op jit(solution)/shard_map/ppermute | solution.py:15
  76.5 3.1 %collective-permute-done.6 = f32[3,64,64]{2,1,0:T(8,128)S(1)} collective-permute-done((f32[3,64,64]{2,1,0:T(8,128)S(1)}, f32[3,64,64]{2,1,0:T(8,128)S(1)}, u32[]{:S(2)}, u32[]{:S(2)}) %collective-permute-start.6) | collective-permute-done | bytes 49184 | tf_op jit(solution)/shard_map/ppermute | solution.py:15
  79.7 2.2 %collective-permute-start.9 = (f32[64,64]{1,0:T(8,128)S(1)}, f32[64,64]{1,0:T(8,128)S(1)}, u32[]{:S(2)}, u32[]{:S(2)}) collective-permute-start(f32[64,64]{1,0:T(8,128)S(1)} %get-tuple-element.7), channel_id=1, source_target_pairs={{0,256},{64,320},{128,384},{192,448},{256,0},{320,64},{384,128},{4... | collective-permute-start | bytes 49160 | tf_op jit(solution)/shard_map/ppermute | solution.py:15
  81.9 0.1 pad_maximum_fusion.1
  82.0 0.0 copy-start.2
  82.0 1.3 %copy.6 = f32[1024,256]{1,0:T(8,128)} copy(f32[1024,256]{0,1:T(8,128)S(1)} %pad_maximum_fusion.1) | data formatting | bytes 2097152
  83.3 3.7 %collective-permute-done.9 = f32[64,64]{1,0:T(8,128)S(1)} collective-permute-done((f32[64,64]{1,0:T(8,128)S(1)}, f32[64,64]{1,0:T(8,128)S(1)}, u32[]{:S(2)}, u32[]{:S(2)}) %collective-permute-start.9) | collective-permute-done | bytes 16416 | tf_op jit(solution)/shard_map/ppermute | solution.py:15
  87.0 0.0 copy-done.2
  87.0 0.7 maximum_multiply_fusion
  (10 shorter events, 0.2 us)
Async XLA Ops:
  0.6 0.9 %copy-start = (bf16[1024,64]{0,1:T(8,128)(2,1)S(1)}, bf16[1024,64]{0,1:T(8,128)(2,1)}, u32[]{:S(2)}) copy-start(bf16[1024,64]{0,1:T(8,128)(2,1)} %param.4) | copy-start | bytes 393220
  0.6 2.6 %copy-start.1 = (bf16[1024,64]{0,1:T(8,128)(2,1)S(1)}, bf16[1024,64]{0,1:T(8,128)(2,1)}, u32[]{:S(2)}) copy-start(bf16[1024,64]{0,1:T(8,128)(2,1)} %param.5) | copy-start | bytes 393220
  3.3 16.9 %collective-permute-start.1 = (bf16[1024,128]{0,1:T(8,128)(2,1)S(1)}, bf16[1024,128]{0,1:T(8,128)(2,1)S(1)}, u32[]{:S(2)}, u32[]{:S(2)}) collective-permute-start(bf16[1024,128]{0,1:T(8,128)(2,1)S(1)} %pad_maximum_fusion.3), channel_id=1, source_target_pairs={{0,128},{64,192},{128,0},{192,64},{256,384},{320,448},{384,256},{4... | collective-permute-start | bytes 786440 | tf_op jit(solution)/shard_map/ppermute | solution.py:15
  8.2 11.9 %collective-permute-start.3 = (bf16[1024,64]{0,1:T(8,128)(2,1)S(1)}, bf16[1024,64]{0,1:T(8,128)(2,1)S(1)}, u32[]{:S(2)}, u32[]{:S(2)}) collective-permute-start(bf16[1024,64]{0,1:T(8,128)(2,1)S(1)} %get-tuple-element.10), channel_id=1, source_target_pairs={{0,256},{64,320},{128,384},{192,448},{256,0},{320,64},{384,128},{4... | collective-permute-start | bytes 393224 | tf_op jit(solution)/shard_map/ppermute | solution.py:15
  12.8 9.5 %collective-permute-start.2 = (bf16[1024,128]{0,1:T(8,128)(2,1)S(1)}, bf16[1024,128]{0,1:T(8,128)(2,1)S(1)}, u32[]{:S(2)}, u32[]{:S(2)}) collective-permute-start(bf16[1024,128]{0,1:T(8,128)(2,1)S(1)} %pad_maximum_fusion.3), channel_id=1, source_target_pairs={{0,192},{64,128},{128,64},{192,0},{256,448},{320,384},{384,320},{4... | collective-permute-start | bytes 786440 | tf_op jit(solution)/shard_map/ppermute | solution.py:15
  14.7 9.7 %collective-permute-start = (bf16[1024,128]{0,1:T(8,128)(2,1)S(1)}, bf16[1024,128]{0,1:T(8,128)(2,1)S(1)}, u32[]{:S(2)}, u32[]{:S(2)}) collective-permute-start(bf16[1024,128]{0,1:T(8,128)(2,1)S(1)} %pad_maximum_fusion.3), channel_id=1, source_target_pairs={{0,64},{64,0},{128,192},{192,128},{256,320},{320,256},{384,448},{4... | collective-permute-start | bytes 786440 | tf_op jit(solution)/shard_map/ppermute | solution.py:15
  24.5 13.4 %collective-permute-start.4 = (bf16[4096,128]{0,1:T(8,128)(2,1)S(1)}, bf16[4096,128]{0,1:T(8,128)(2,1)}, u32[]{:S(2)}, u32[]{:S(2)}) collective-permute-start(bf16[4096,128]{0,1:T(8,128)(2,1)S(1)} %pad_maximum_fusion), channel_id=1, source_target_pairs={{0,1},{1,0},{2,3},{3,2},{4,5},{5,4},{6,7},{7,6},{8,9},{9,8},{10,11... | collective-permute-start | bytes 3145736 | tf_op jit(solution)/shard_map/ppermute | solution.py:15
  46.7 17.7 %collective-permute-start.5 = (f32[1024,128]{0,1:T(8,128)S(1)}, f32[1024,128]{0,1:T(8,128)S(1)}, u32[]{:S(2)}, u32[]{:S(2)}) collective-permute-start(f32[1024,128]{0,1:T(8,128)S(1)} %pad_maximum_fusion.2), channel_id=1, source_target_pairs={{0,256},{64,320},{128,384},{192,448},{256,0},{320,64},{384,128},{4... | collective-permute-start | bytes 1572872 | tf_op jit(solution)/shard_map/ppermute | solution.py:15
  65.2 10.2 %collective-permute-start.8 = (f32[2,64,64]{2,1,0:T(8,128)S(1)}, f32[2,64,64]{2,1,0:T(8,128)S(1)}, u32[]{:S(2)}, u32[]{:S(2)}) collective-permute-start(f32[2,64,64]{2,1,0:T(8,128)S(1)} %pad_maximum_fusion.5), channel_id=1, source_target_pairs={{0,192},{64,128},{128,64},{192,0},{256,448},{320,384},{384,320},{4... | collective-permute-start | bytes 98312 | tf_op jit(solution)/shard_map/ppermute | solution.py:15
  68.9 7.7 %collective-permute-start.7 = (f32[2,64,64]{2,1,0:T(8,128)S(1)}, f32[2,64,64]{2,1,0:T(8,128)S(1)}, u32[]{:S(2)}, u32[]{:S(2)}) collective-permute-start(f32[2,64,64]{2,1,0:T(8,128)S(1)} %pad_maximum_fusion.5), channel_id=1, source_target_pairs={{0,128},{64,192},{128,0},{192,64},{256,384},{320,448},{384,256},{4... | collective-permute-start | bytes 98312 | tf_op jit(solution)/shard_map/ppermute | solution.py:15
  73.1 6.5 %collective-permute-start.6 = (f32[3,64,64]{2,1,0:T(8,128)S(1)}, f32[3,64,64]{2,1,0:T(8,128)S(1)}, u32[]{:S(2)}, u32[]{:S(2)}) collective-permute-start(f32[3,64,64]{2,1,0:T(8,128)S(1)} %pad_maximum_fusion.4), channel_id=1, source_target_pairs={{0,64},{64,0},{128,192},{192,128},{256,320},{320,256},{384,448},{4... | collective-permute-start | bytes 147464 | tf_op jit(solution)/shard_map/ppermute | solution.py:15
  79.7 7.3 %collective-permute-start.9 = (f32[64,64]{1,0:T(8,128)S(1)}, f32[64,64]{1,0:T(8,128)S(1)}, u32[]{:S(2)}, u32[]{:S(2)}) collective-permute-start(f32[64,64]{1,0:T(8,128)S(1)} %get-tuple-element.7), channel_id=1, source_target_pairs={{0,256},{64,320},{128,384},{192,448},{256,0},{320,64},{384,128},{4... | collective-permute-start | bytes 49160 | tf_op jit(solution)/shard_map/ppermute | solution.py:15
  82.0 5.0 %copy-start.2 = (f32[4]{0:T(128)S(1)}, f32[4]{0:T(128)}, u32[]{:S(2)}) copy-start(f32[4]{0:T(128)} %constant.7) | copy-start | bytes 52
where the time goes:
time: 88.2 us; the launch traced here: 87.7 us
  starting transfers between devices  34 us (39%)
  matrix products  28.8 us (33%)
  waiting for transfers between devices  19.2 us (22%)
  other arithmetic  2.51 us (3%)
  local copies, waits for them, and re-layouts  2.25 us (3%)
  between operations  0.91 us (1%)
    ppermute x10, starting transfers between devices, exchanged(): return lax.ppermute(value, axis, pairs)  34 us
    dot_general x5, matrix products, raw_product(): return jnp.dot(kernel, col_sketch, preferred_element_type=jnp.float32)  25.7 us
    ppermute x10, waiting for transfers between devices, exchanged(): return lax.ppermute(value, axis, pairs)  19.2 us
    unnamed x8, local copies, waits for them, and re-layouts  2.23 us
  transfers between devices with their start and end apart: 10, of which 6 were waited for; matrix products, arithmetic and copies ran while one was open for 24% of the time, Pallas kernels for 0%

commit v1 on v0

--- a/solution.py
+++ b/solution.py
@@ -55,9 +55,7 @@
     results = []
     grams = []
     for tier_num in range(top):
-        sibs = [
-            exchanged(packed, "leaf", mask) for mask in range(1 << tier_num, 2 << tier_num)
-        ]
+        sibs = [exchanged(packed, "leaf", mask) for mask in range(1 << tier_num, 2 << tier_num)]
         sib = jnp.concatenate(sibs) if len(sibs) > 1 else sibs[0]
         product = raw_product(located, row_sq, sib, dim) / math.sqrt(sib.shape[0])
         results.append(product)
@@ -81,9 +79,11 @@
         part = lax.optimization_barrier(raw_product(located, row_sq, piece, dim))
         own_far = part if own_far is None else own_far + part
         far_rows += piece.shape[0]
+    far_back = swapped(own_far, "leaf", top)
     product = (own_far + back[:, rank:]) / math.sqrt(2 * far_rows)
     results.append(product)
-    grams.append(gram_of(product))
+    mirror = (far_back + partner_far) / math.sqrt(2 * far_rows)
+    grams.append(gram_of(product) + gram_of(mirror))
     low = 1 << top
     pair_sum = grams[1]
     quad_sum = [grams[2], grams[3]]
@@ -95,8 +95,7 @@
         else:
             got = exchanged(jnp.stack(grams[2:]), "leaf", mask)
         quad_sum = [quad_sum[0] + got[0], quad_sum[1] + got[1]]
-    last = quad_sum[1] + exchanged(quad_sum[1], "leaf", low)
-    done = [grams[0], pair_sum, quad_sum[0], last]
+    done = [grams[0], pair_sum, quad_sum[0], quad_sum[1]]
     stacked = jnp.stack(done)
     divisors = jnp.asarray(
         [float((1 << tier_num) * rows_n) for tier_num in range(len(grams))], jnp.float32

time: 88.2 us -> 91.4 us (1.036)
  the two profiles are of different devices: /device:TPU:16 before, /device:TPU:1 now
where the time goes in v1:
time: 91.4 us; the launch traced here: 90.9 us
  starting transfers between devices  35.3 us (39%)
  matrix products  29.2 us (32%)
  waiting for transfers between devices  20.6 us (23%)
  other arithmetic  2.51 us (3%)
  local copies, waits for them, and re-layouts  2.25 us (2%)
  between operations  0.92 us (1%)
    ppermute x10, starting transfers between devices, exchanged(): return lax.ppermute(value, axis, pairs)  35.3 us
    dot_general x5, matrix products, raw_product(): return jnp.dot(kernel, col_sketch, preferred_element_type=jnp.float32)  25.7 us
    ppermute x10, waiting for transfers between devices, exchanged(): return lax.ppermute(value, axis, pairs)  20.6 us
    unnamed x8, local copies, waits for them, and re-layouts  2.23 us
  transfers between devices with their start and end apart: 10, of which 4 were waited for; matrix products, arithmetic and copies ran while one was open for 23% of the time, Pallas kernels for 0%

profile of v1, /device:TPU:1, one launch (start us, length us, event | category | flops | bytes accessed | tf_op | source)
XLA Modules:
  0.0 90.9 jit_solution(10014552089612533000)
XLA Ops:
  0.6 0.0 copy-start
  0.6 0.0 copy-start.1
  0.7 0.9 copy-done
  1.5 1.7 %multiply_reduce_fusion.5 = (f32[1024]{0:T(1024)S(1)}, bf16[1024,64]{0,1:T(8,128)(2,1)S(1)}) fusion(bf16[1024,64]{0,1:T(8,128)(2,1)S(1)} %copy-done, s32[1024]{0:T(1024)} %bitcast.71), kind=kOutput, calls=%fused_computation.40 | convolution fusion | flops 135527424 | bytes 270336 | tf_op jit(solution)/shard_map/dot_general | solution.py:44
  3.3 0.0 copy-done.1
  3.3 5.5 %collective-permute-start.1 = (bf16[1024,128]{0,1:T(8,128)(2,1)S(1)}, bf16[1024,128]{0,1:T(8,128)(2,1)S(1)}, u32[]{:S(2)}, u32[]{:S(2)}) collective-permute-start(bf16[1024,128]{0,1:T(8,128)(2,1)S(1)} %pad_maximum_fusion.3), channel_id=1, source_target_pairs={{0,128},{64,192},{128,0},{192,64},{256,384},{320,448},{384,256},{4... | collective-permute-start | bytes 786440 | tf_op jit(solution)/shard_map/ppermute | solution.py:15
  8.8 4.8 %collective-permute-start.3 = (bf16[1024,64]{0,1:T(8,128)(2,1)S(1)}, bf16[1024,64]{0,1:T(8,128)(2,1)S(1)}, u32[]{:S(2)}, u32[]{:S(2)}) collective-permute-start(bf16[1024,64]{0,1:T(8,128)(2,1)S(1)} %get-tuple-element.10), channel_id=1, source_target_pairs={{0,256},{64,320},{128,384},{192,448},{256,0},{320,64},{384,128},{4... | collective-permute-start | bytes 393224 | tf_op jit(solution)/shard_map/ppermute | solution.py:15
  13.6 2.8 %collective-permute-start.2 = (bf16[1024,128]{0,1:T(8,128)(2,1)S(1)}, bf16[1024,128]{0,1:T(8,128)(2,1)S(1)}, u32[]{:S(2)}, u32[]{:S(2)}) collective-permute-start(bf16[1024,128]{0,1:T(8,128)(2,1)S(1)} %pad_maximum_fusion.3), channel_id=1, source_target_pairs={{0,192},{64,128},{128,64},{192,0},{256,448},{320,384},{384,320},{4... | collective-permute-start | bytes 786440 | tf_op jit(solution)/shard_map/ppermute | solution.py:15
  16.4 1.9 %collective-permute-start = (bf16[1024,128]{0,1:T(8,128)(2,1)S(1)}, bf16[1024,128]{0,1:T(8,128)(2,1)S(1)}, u32[]{:S(2)}, u32[]{:S(2)}) collective-permute-start(bf16[1024,128]{0,1:T(8,128)(2,1)S(1)} %pad_maximum_fusion.3), channel_id=1, source_target_pairs={{0,64},{64,0},{128,192},{192,128},{256,320},{320,256},{384,448},{4... | collective-permute-start | bytes 786440 | tf_op jit(solution)/shard_map/ppermute | solution.py:15
  18.3 0.0 collective-permute-done.3
  18.4 0.0 collective-permute-done.1
  18.4 5.1 %collective-permute-done.2 = bf16[1024,128]{0,1:T(8,128)(2,1)S(1)} collective-permute-done((bf16[1024,128]{0,1:T(8,128)(2,1)S(1)}, bf16[1024,128]{0,1:T(8,128)(2,1)S(1)}, u32[]{:S(2)}, u32[]{:S(2)}) %collective-permute-start.2) | collective-permute-done | bytes 262176 | tf_op jit(solution)/shard_map/ppermute | solution.py:15
  23.5 0.1 multiply_reduce_fusion.2
  23.6 1.0 %collective-permute-done = bf16[1024,128]{0,1:T(8,128)(2,1)S(1)} collective-permute-done((bf16[1024,128]{0,1:T(8,128)(2,1)S(1)}, bf16[1024,128]{0,1:T(8,128)(2,1)S(1)}, u32[]{:S(2)}, u32[]{:S(2)}) %collective-permute-start) | collective-permute-done | bytes 262176 | tf_op jit(solution)/shard_map/ppermute | solution.py:15
  24.6 0.1 pad_maximum_fusion
  24.7 4.3 %collective-permute-start.4 = (bf16[4096,128]{0,1:T(8,128)(2,1)S(1)}, bf16[4096,128]{0,1:T(8,128)(2,1)}, u32[]{:S(2)}, u32[]{:S(2)}) collective-permute-start(bf16[4096,128]{0,1:T(8,128)(2,1)S(1)} %pad_maximum_fusion), channel_id=1, source_target_pairs={{0,1},{1,0},{2,3},{3,2},{4,5},{5,4},{6,7},{7,6},{8,9},{9,8},{10,11... | collective-permute-start | bytes 3145736 | tf_op jit(solution)/shard_map/ppermute | solution.py:15
  29.0 3.2 %fusion.8 = f32[1024,64]{0,1:T(8,128)S(1)} fusion(bf16[1024,64]{0,1:T(8,128)(2,1)S(1)} %get-tuple-element.10, f32[2048]{0:T(1024)S(1)} %multiply_reduce_fusion.2, f32[1024]{0:T(1024)S(1)} %get-tuple-element.9, bf16[2048,128]{0,1:T(8,128)(2,1)S(1)} %constant_dynamic-update-slice_fusion), kind=kOutput, calls=%fused_computation.14 | convolution fusion | flops 549519360 | bytes 929792 | tf_op jit(solution)/shard_map/dot_general | solution.py:31
  32.2 1.7 %fusion.7 = f32[1024,64]{0,1:T(8,128)S(1)} fusion(bf16[1024,64]{0,1:T(8,128)(2,1)S(1)} %get-tuple-element.10, f32[1024]{0:T(1024)S(1)} %multiply_reduce_fusion.4, f32[1024]{0:T(1024)S(1)} %get-tuple-element.9, bf16[1024,128]{0,1:T(8,128)(2,1)S(1)} %collective-permute-done), kind=kOutput, calls=%fused_computation.13 | convolution fusion | flops 274792448 | bytes 663552 | tf_op jit(solution)/shard_map/dot_general | solution.py:31
  33.9 0.1 multiply_reduce_fusion.1
  34.0 6.1 %fusion.2 = f32[1024,64]{0,1:T(8,128)S(1)} fusion(bf16[1024,64]{0,1:T(8,128)(2,1)S(1)} %collective-permute-done.3, f32[4096]{0:T(1024)S(1)} %multiply_reduce_fusion.1, f32[1024]{0:T(1024)S(1)} %multiply_reduce_fusion.3, bf16[4096,128]{0,1:T(8,128)(2,1)S(1)} %pad_maximum_fusion), kind=kOutput, calls=%fused_computation.8 | convolution fusion | flops 1098907648 | bytes 1462272 | tf_op jit(solution)/shard_map/dot_general | solution.py:31
  40.1 0.0 collective-permute-done.4
  40.1 1.2 %multiply_reduce_fusion = f32[4096]{0:T(1024)S(1)} fusion(bf16[4096,128]{0,1:T(8,128)(2,1)} %collective-permute-done.4), kind=kLoop, calls=%fused_computation.20 | loop fusion | flops 782336 | bytes 540672 | tf_op jit(solution)/shard_map/reduce_sum | solution.py:19
  41.3 7.5 %fusion.4 = f32[1024,64]{0,1:T(8,128)S(1)} fusion(bf16[1024,64]{0,1:T(8,128)(2,1)S(1)} %get-tuple-element.10, f32[1024]{0:T(1024)S(1)} %get-tuple-element.9, f32[4096]{0:T(1024)S(1)} %multiply_reduce_fusion, bf16[4096,128]{0,1:T(8,128)(2,1)} %collective-permute-done.4), kind=kOutput, calls=%fused_computation.10 | convolution fusion | flops 1098907648 | bytes 1462272 | tf_op jit(solution)/shard_map/dot_general | solution.py:31
  48.8 3.8 %collective-permute-start.6 = (f32[1024,64]{0,1:T(8,128)S(1)}, f32[1024,64]{0,1:T(8,128)S(1)}, u32[]{:S(2)}, u32[]{:S(2)}) collective-permute-start(f32[1024,64]{0,1:T(8,128)S(1)} %fusion.4), channel_id=1, source_target_pairs={{0,256},{64,320},{128,384},{192,448},{256,0},{320,64},{384,128},{4... | collective-permute-start | bytes 786440 | tf_op jit(solution)/shard_map/ppermute | solution.py:15
  52.6 7.3 %fusion.3 = f32[1024,64]{0,1:T(8,128)S(1)} fusion(bf16[1024,64]{0,1:T(8,128)(2,1)S(1)} %collective-permute-done.3, f32[4096]{0:T(1024)S(1)} %multiply_reduce_fusion, f32[1024]{0:T(1024)S(1)} %multiply_reduce_fusion.3, bf16[4096,128]{0,1:T(8,128)(2,1)} %collective-permute-done.4), kind=kOutput, calls=%fused_computation.9 | convolution fusion | flops 1098907648 | bytes 1462272 | tf_op jit(solution)/shard_map/dot_general | solution.py:31
  59.9 3.0 %collective-permute-start.5 = (f32[1024,128]{0,1:T(8,128)S(1)}, f32[1024,128]{0,1:T(8,128)S(1)}, u32[]{:S(2)}, u32[]{:S(2)}) collective-permute-start(f32[1024,128]{0,1:T(8,128)S(1)} %pad_maximum_fusion.2), channel_id=1, source_target_pairs={{0,256},{64,320},{128,384},{192,448},{256,0},{320,64},{384,128},{4... | collective-permute-start | bytes 1572872 | tf_op jit(solution)/shard_map/ppermute | solution.py:15
  62.9 0.4 convolution_bitcast_fusion
  63.3 0.4 fusion.57
  63.7 0.0 collective-permute-done.6
  63.7 0.4 fusion.21
  64.1 12.5 %collective-permute-done.5 = f32[1024,128]{0,1:T(8,128)S(1)} collective-permute-done((f32[1024,128]{0,1:T(8,128)S(1)}, f32[1024,128]{0,1:T(8,128)S(1)}, u32[]{:S(2)}, u32[]{:S(2)}) %collective-permute-start.5) | collective-permute-done | bytes 524320 | tf_op jit(solution)/shard_map/ppermute | solution.py:15
  76.5 0.1 slice_multiply_fusion
  76.6 0.4 convolution_add_fusion
  77.0 0.4 fusion.56
  77.4 3.4 %collective-permute-start.9 = (f32[2,64,64]{2,1,0:T(8,128)S(1)}, f32[2,64,64]{2,1,0:T(8,128)S(1)}, u32[]{:S(2)}, u32[]{:S(2)}) collective-permute-start(f32[2,64,64]{2,1,0:T(8,128)S(1)} %pad_maximum_fusion.5), channel_id=1, source_target_pairs={{0,192},{64,128},{128,64},{192,0},{256,448},{320,384},{384,320},{4... | collective-permute-start | bytes 98312 | tf_op jit(solution)/shard_map/ppermute | solution.py:15
  80.7 4.0 %collective-permute-start.8 = (f32[2,64,64]{2,1,0:T(8,128)S(1)}, f32[2,64,64]{2,1,0:T(8,128)S(1)}, u32[]{:S(2)}, u32[]{:S(2)}) collective-permute-start(f32[2,64,64]{2,1,0:T(8,128)S(1)} %pad_maximum_fusion.5), channel_id=1, source_target_pairs={{0,128},{64,192},{128,0},{192,64},{256,384},{320,448},{384,256},{4... | collective-permute-start | bytes 98312 | tf_op jit(solution)/shard_map/ppermute | solution.py:15
  84.7 1.9 %collective-permute-start.7 = (f32[3,64,64]{2,1,0:T(8,128)S(1)}, f32[3,64,64]{2,1,0:T(8,128)S(1)}, u32[]{:S(2)}, u32[]{:S(2)}) collective-permute-start(f32[3,64,64]{2,1,0:T(8,128)S(1)} %pad_maximum_fusion.4), channel_id=1, source_target_pairs={{0,64},{64,0},{128,192},{192,128},{256,320},{320,256},{384,448},{4... | collective-permute-start | bytes 147464 | tf_op jit(solution)/shard_map/ppermute | solution.py:15
  86.7 0.1 pad_maximum_fusion.1
  86.8 0.0 copy-start.2
  86.8 1.3 %copy.6 = f32[1024,256]{1,0:T(8,128)} copy(f32[1024,256]{0,1:T(8,128)S(1)} %pad_maximum_fusion.1) | data formatting | bytes 2097152
  88.1 0.0 collective-permute-done.9
  88.1 0.0 collective-permute-done.8
  88.1 2.0 %collective-permute-done.7 = f32[3,64,64]{2,1,0:T(8,128)S(1)} collective-permute-done((f32[3,64,64]{2,1,0:T(8,128)S(1)}, f32[3,64,64]{2,1,0:T(8,128)S(1)}, u32[]{:S(2)}, u32[]{:S(2)}) %collective-permute-start.7) | collective-permute-done | bytes 49184 | tf_op jit(solution)/shard_map/ppermute | solution.py:15
  90.1 0.0 copy-done.2
  90.1 0.7 maximum_multiply_fusion
  (9 shorter events, 0.2 us)
Async XLA Ops:
  0.6 0.9 %copy-start = (bf16[1024,64]{0,1:T(8,128)(2,1)S(1)}, bf16[1024,64]{0,1:T(8,128)(2,1)}, u32[]{:S(2)}) copy-start(bf16[1024,64]{0,1:T(8,128)(2,1)} %param.4) | copy-start | bytes 393220
  0.6 2.6 %copy-start.1 = (bf16[1024,64]{0,1:T(8,128)(2,1)S(1)}, bf16[1024,64]{0,1:T(8,128)(2,1)}, u32[]{:S(2)}) copy-start(bf16[1024,64]{0,1:T(8,128)(2,1)} %param.5) | copy-start | bytes 393220
  3.3 15.1 %collective-permute-start.1 = (bf16[1024,128]{0,1:T(8,128)(2,1)S(1)}, bf16[1024,128]{0,1:T(8,128)(2,1)S(1)}, u32[]{:S(2)}, u32[]{:S(2)}) collective-permute-start(bf16[1024,128]{0,1:T(8,128)(2,1)S(1)} %pad_maximum_fusion.3), channel_id=1, source_target_pairs={{0,128},{64,192},{128,0},{192,64},{256,384},{320,448},{384,256},{4... | collective-permute-start | bytes 786440 | tf_op jit(solution)/shard_map/ppermute | solution.py:15
  8.8 9.5 %collective-permute-start.3 = (bf16[1024,64]{0,1:T(8,128)(2,1)S(1)}, bf16[1024,64]{0,1:T(8,128)(2,1)S(1)}, u32[]{:S(2)}, u32[]{:S(2)}) collective-permute-start(bf16[1024,64]{0,1:T(8,128)(2,1)S(1)} %get-tuple-element.10), channel_id=1, source_target_pairs={{0,256},{64,320},{128,384},{192,448},{256,0},{320,64},{384,128},{4... | collective-permute-start | bytes 393224 | tf_op jit(solution)/shard_map/ppermute | solution.py:15
  13.6 9.9 %collective-permute-start.2 = (bf16[1024,128]{0,1:T(8,128)(2,1)S(1)}, bf16[1024,128]{0,1:T(8,128)(2,1)S(1)}, u32[]{:S(2)}, u32[]{:S(2)}) collective-permute-start(bf16[1024,128]{0,1:T(8,128)(2,1)S(1)} %pad_maximum_fusion.3), channel_id=1, source_target_pairs={{0,192},{64,128},{128,64},{192,0},{256,448},{320,384},{384,320},{4... | collective-permute-start | bytes 786440 | tf_op jit(solution)/shard_map/ppermute | solution.py:15
  16.4 8.2 %collective-permute-start = (bf16[1024,128]{0,1:T(8,128)(2,1)S(1)}, bf16[1024,128]{0,1:T(8,128)(2,1)S(1)}, u32[]{:S(2)}, u32[]{:S(2)}) collective-permute-start(bf16[1024,128]{0,1:T(8,128)(2,1)S(1)} %pad_maximum_fusion.3), channel_id=1, source_target_pairs={{0,64},{64,0},{128,192},{192,128},{256,320},{320,256},{384,448},{4... | collective-permute-start | bytes 786440 | tf_op jit(solution)/shard_map/ppermute | solution.py:15
  24.7 15.4 %collective-permute-start.4 = (bf16[4096,128]{0,1:T(8,128)(2,1)S(1)}, bf16[4096,128]{0,1:T(8,128)(2,1)}, u32[]{:S(2)}, u32[]{:S(2)}) collective-permute-start(bf16[4096,128]{0,1:T(8,128)(2,1)S(1)} %pad_maximum_fusion), channel_id=1, source_target_pairs={{0,1},{1,0},{2,3},{3,2},{4,5},{5,4},{6,7},{7,6},{8,9},{9,8},{10,11... | collective-permute-start | bytes 3145736 | tf_op jit(solution)/shard_map/ppermute | solution.py:15
  48.8 14.9 %collective-permute-start.6 = (f32[1024,64]{0,1:T(8,128)S(1)}, f32[1024,64]{0,1:T(8,128)S(1)}, u32[]{:S(2)}, u32[]{:S(2)}) collective-permute-start(f32[1024,64]{0,1:T(8,128)S(1)} %fusion.4), channel_id=1, source_target_pairs={{0,256},{64,320},{128,384},{192,448},{256,0},{320,64},{384,128},{4... | collective-permute-start | bytes 786440 | tf_op jit(solution)/shard_map/ppermute | solution.py:15
  59.9 16.6 %collective-permute-start.5 = (f32[1024,128]{0,1:T(8,128)S(1)}, f32[1024,128]{0,1:T(8,128)S(1)}, u32[]{:S(2)}, u32[]{:S(2)}) collective-permute-start(f32[1024,128]{0,1:T(8,128)S(1)} %pad_maximum_fusion.2), channel_id=1, source_target_pairs={{0,256},{64,320},{128,384},{192,448},{256,0},{320,64},{384,128},{4... | collective-permute-start | bytes 1572872 | tf_op jit(solution)/shard_map/ppermute | solution.py:15
  77.4 10.7 %collective-permute-start.9 = (f32[2,64,64]{2,1,0:T(8,128)S(1)}, f32[2,64,64]{2,1,0:T(8,128)S(1)}, u32[]{:S(2)}, u32[]{:S(2)}) collective-permute-start(f32[2,64,64]{2,1,0:T(8,128)S(1)} %pad_maximum_fusion.5), channel_id=1, source_target_pairs={{0,192},{64,128},{128,64},{192,0},{256,448},{320,384},{384,320},{4... | collective-permute-start | bytes 98312 | tf_op jit(solution)/shard_map/ppermute | solution.py:15
  80.7 7.3 %collective-permute-start.8 = (f32[2,64,64]{2,1,0:T(8,128)S(1)}, f32[2,64,64]{2,1,0:T(8,128)S(1)}, u32[]{:S(2)}, u32[]{:S(2)}) collective-permute-start(f32[2,64,64]{2,1,0:T(8,128)S(1)} %pad_maximum_fusion.5), channel_id=1, source_target_pairs={{0,128},{64,192},{128,0},{192,64},{256,384},{320,448},{384,256},{4... | collective-permute-start | bytes 98312 | tf_op jit(solution)/shard_map/ppermute | solution.py:15
  84.7 5.4 %collective-permute-start.7 = (f32[3,64,64]{2,1,0:T(8,128)S(1)}, f32[3,64,64]{2,1,0:T(8,128)S(1)}, u32[]{:S(2)}, u32[]{:S(2)}) collective-permute-start(f32[3,64,64]{2,1,0:T(8,128)S(1)} %pad_maximum_fusion.4), channel_id=1, source_target_pairs={{0,64},{64,0},{128,192},{192,128},{256,320},{320,256},{384,448},{4... | collective-permute-start | bytes 147464 | tf_op jit(solution)/shard_map/ppermute | solution.py:15
  86.8 3.4 %copy-start.2 = (f32[4]{0:T(128)S(1)}, f32[4]{0:T(128)}, u32[]{:S(2)}) copy-start(f32[4]{0:T(128)} %constant.30) | copy-start | bytes 52

commit v2 on v1

--- a/solution.py
+++ b/solution.py
@@ -50,20 +50,24 @@
     top = leaf_bits - 1
     y_rows = swapped(located, "leaf", top)
     y_sq = squares_of(y_rows)
+    partner_own = lax.optimization_barrier(raw_product(y_rows, y_sq, packed, dim))
     cluster = [packed]
     other_pieces = []
     results = []
     grams = []
     for tier_num in range(top):
-        sibs = [exchanged(packed, "leaf", mask) for mask in range(1 << tier_num, 2 << tier_num)]
+        sibs = [
+            exchanged(packed, "leaf", mask) for mask in range(1 << tier_num, 2 << tier_num)
+        ]
         sib = jnp.concatenate(sibs) if len(sibs) > 1 else sibs[0]
         product = raw_product(located, row_sq, sib, dim) / math.sqrt(sib.shape[0])
         results.append(product)
         grams.append(gram_of(product))
         cluster.append(sib)
+    received = jnp.concatenate(cluster[1:])
     cluster = jnp.concatenate(cluster)
     other_pieces = [swapped(cluster, "pair", 0)]
-    partner_near = raw_product(y_rows, y_sq, cluster, dim)
+    partner_near = partner_own + raw_product(y_rows, y_sq, received, dim)
     partner_far = None
     for piece in other_pieces:
         part = raw_product(y_rows, y_sq, piece, dim)

time: 91.4 us -> 95.5 us (1.045)
  the two profiles are of different devices: /device:TPU:1 before, /device:TPU:504 now
where the time goes in v2:
time: 95.5 us; the launch traced here: 95 us
  starting transfers between devices  32.2 us (34%)
  matrix products  30.9 us (32%)
  waiting for transfers between devices  25.1 us (26%)
  other arithmetic  3.45 us (4%)
  local copies, waits for them, and re-layouts  2.34 us (2%)
    ppermute x10, starting transfers between devices, exchanged(): return lax.ppermute(value, axis, pairs)  32.2 us
    dot_general x6, matrix products, raw_product(): return jnp.dot(kernel, col_sketch, preferred_element_type=jnp.float32)  27.4 us
    ppermute x10, waiting for transfers between devices, exchanged(): return lax.ppermute(value, axis, pairs)  25.1 us
    unnamed x11, local copies, waits for them, and re-layouts  2.29 us
  transfers between devices with their start and end apart: 10, of which 4 were waited for; matrix products, arithmetic and copies ran while one was open for 25% of the time, Pallas kernels for 0%

profile of v2, /device:TPU:504, one launch (start us, length us, event | category | flops | bytes accessed | tf_op | source)
XLA Modules:
  0.0 95.0 jit_solution(328454131935000178)
XLA Ops:
  0.6 0.0 copy-start
  0.6 0.0 copy-start.1
  0.7 0.9 copy-done
  1.5 1.7 %multiply_reduce_fusion.5 = (f32[1024]{0:T(1024)S(1)}, bf16[1024,64]{0,1:T(8,128)(2,1)S(1)}) fusion(bf16[1024,64]{0,1:T(8,128)(2,1)S(1)} %copy-done, s32[1024]{0:T(1024)} %bitcast.74), kind=kOutput, calls=%fused_computation.42 | convolution fusion | flops 135527424 | bytes 270336 | tf_op jit(solution)/shard_map/dot_general | solution.py:44
  3.3 3.1 %collective-permute-start.3 = (bf16[1024,64]{0,1:T(8,128)(2,1)S(1)}, bf16[1024,64]{0,1:T(8,128)(2,1)S(1)}, u32[]{:S(2)}, u32[]{:S(2)}) collective-permute-start(bf16[1024,64]{0,1:T(8,128)(2,1)S(1)} %get-tuple-element.14), channel_id=1, source_target_pairs={{0,256},{64,320},{128,384},{192,448},{256,0},{320,64},{384,128},{4... | collective-permute-start | bytes 393224 | tf_op jit(solution)/shard_map/ppermute | solution.py:15
  6.4 3.4 %collective-permute-start = (bf16[1024,128]{0,1:T(8,128)(2,1)S(1)}, bf16[1024,128]{0,1:T(8,128)(2,1)S(1)}, u32[]{:S(2)}, u32[]{:S(2)}) collective-permute-start(bf16[1024,128]{0,1:T(8,128)(2,1)S(1)} %pad_maximum_fusion.3), channel_id=1, source_target_pairs={{0,64},{64,0},{128,192},{192,128},{256,320},{320,256},{384,448},{4... | collective-permute-start | bytes 786440 | tf_op jit(solution)/shard_map/ppermute | solution.py:15
  9.8 4.6 %collective-permute-start.1 = (bf16[1024,128]{0,1:T(8,128)(2,1)S(1)}, bf16[1024,128]{0,1:T(8,128)(2,1)S(1)}, u32[]{:S(2)}, u32[]{:S(2)}) collective-permute-start(bf16[1024,128]{0,1:T(8,128)(2,1)S(1)} %pad_maximum_fusion.3), channel_id=1, source_target_pairs={{0,128},{64,192},{128,0},{192,64},{256,384},{320,448},{384,256},{4... | collective-permute-start | bytes 786440 | tf_op jit(solution)/shard_map/ppermute | solution.py:15
  14.5 2.4 %collective-permute-start.2 = (bf16[1024,128]{0,1:T(8,128)(2,1)S(1)}, bf16[1024,128]{0,1:T(8,128)(2,1)S(1)}, u32[]{:S(2)}, u32[]{:S(2)}) collective-permute-start(bf16[1024,128]{0,1:T(8,128)(2,1)S(1)} %pad_maximum_fusion.3), channel_id=1, source_target_pairs={{0,192},{64,128},{128,64},{192,0},{256,448},{320,384},{384,320},{4... | collective-permute-start | bytes 786440 | tf_op jit(solution)/shard_map/ppermute | solution.py:15
  16.9 0.0 collective-permute-done.3
  16.9 2.4 %fusion.7 = f32[1024,64]{0,1:T(8,128)} fusion(bf16[1024,64]{0,1:T(8,128)(2,1)S(1)} %copy-done.1, bf16[1024,64]{0,1:T(8,128)(2,1)S(1)} %collective-permute-done.3, bf16[1024,64]{0,1:T(8,128)(2,1)S(1)} %get-tuple-element.14, f32[1024]{0:T(1024)S(1)} %get-tuple-element.13, f32[1024]{0:T(1024)S(1)} %multiply_reduce_fusion.3), kind=kOutput, calls=%fused_computation.14 | convolution fusion | flops 274726912 | bytes 663552 | tf_op jit(solution)/shard_map/dot_general | solution.py:31
  19.4 0.0 collective-permute-done
  19.4 4.7 %collective-permute-done.1 = bf16[1024,128]{0,1:T(8,128)(2,1)S(1)} collective-permute-done((bf16[1024,128]{0,1:T(8,128)(2,1)S(1)}, bf16[1024,128]{0,1:T(8,128)(2,1)S(1)}, u32[]{:S(2)}, u32[]{:S(2)}) %collective-permute-start.1) | collective-permute-done | bytes 262176 | tf_op jit(solution)/shard_map/ppermute | solution.py:15
  24.0 5.3 %collective-permute-done.2 = bf16[1024,128]{0,1:T(8,128)(2,1)S(1)} collective-permute-done((bf16[1024,128]{0,1:T(8,128)(2,1)S(1)}, bf16[1024,128]{0,1:T(8,128)(2,1)S(1)}, u32[]{:S(2)}, u32[]{:S(2)}) %collective-permute-start.2) | collective-permute-done | bytes 262176 | tf_op jit(solution)/shard_map/ppermute | solution.py:15
  29.3 0.1 pad_maximum_fusion
  29.3 2.1 %collective-permute-start.4 = (bf16[4096,128]{0,1:T(8,128)(2,1)S(1)}, bf16[4096,128]{0,1:T(8,128)(2,1)}, u32[]{:S(2)}, u32[]{:S(2)}) collective-permute-start(bf16[4096,128]{0,1:T(8,128)(2,1)S(1)} %pad_maximum_fusion), channel_id=1, source_target_pairs={{0,1},{1,0},{2,3},{3,2},{4,5},{5,4},{6,7},{7,6},{8,9},{9,8},{10,11... | collective-permute-start | bytes 3145736 | tf_op jit(solution)/shard_map/ppermute | solution.py:15
  31.5 0.1 constant_dynamic-update-slice_fusion.1
  31.5 0.1 constant_dynamic-update-slice_fusion
  31.6 0.1 multiply_reduce_fusion.1
  31.7 0.0 copy-start.2
  31.7 5.4 %fusion.4 = f32[1024,64]{0,1:T(8,128)} fusion(bf16[1024,64]{0,1:T(8,128)(2,1)S(1)} %collective-permute-done.3, f32[3072]{0:T(1024)S(1)} %multiply_reduce_fusion.1, f32[1024]{0:T(1024)S(1)} %multiply_reduce_fusion.3, bf16[3072,128]{0,1:T(8,128)(2,1)S(1)} %get-tuple-element.7), kind=kOutput, calls=%fused_computation.11 | convolution fusion | flops 824180736 | bytes 1196032 | tf_op jit(solution)/shard_map/dot_general | solution.py:31
  37.1 1.0 %add.121 = f32[1024,64]{0,1:T(8,128)S(1)} add(f32[1024,64]{0,1:T(8,128)S(1)} %copy-done.2, f32[1024,64]{0,1:T(8,128)} %fusion.4) | non-fusion elementwise | flops 65536 | bytes 786432 | tf_op jit(solution)/shard_map/add | solution.py:70
  38.1 0.1 multiply_reduce_fusion.2
  38.2 1.7 %fusion.8 = f32[1024,64]{0,1:T(8,128)S(1)} fusion(bf16[1024,64]{0,1:T(8,128)(2,1)S(1)} %get-tuple-element.14, f32[1024]{0:T(1024)S(1)} %multiply_reduce_fusion.4, f32[1024]{0:T(1024)S(1)} %get-tuple-element.13, bf16[1024,128]{0,1:T(8,128)(2,1)S(1)} %collective-permute-done), kind=kOutput, calls=%fused_computation.15 | convolution fusion | flops 274792448 | bytes 663552 | tf_op jit(solution)/shard_map/dot_general | solution.py:31
  39.9 3.2 %fusion.9 = f32[1024,64]{0,1:T(8,128)S(1)} fusion(bf16[1024,64]{0,1:T(8,128)(2,1)S(1)} %get-tuple-element.14, f32[2048]{0:T(1024)S(1)} %multiply_reduce_fusion.2, f32[1024]{0:T(1024)S(1)} %get-tuple-element.13, bf16[2048,128]{0,1:T(8,128)(2,1)S(1)} %get-tuple-element.6), kind=kOutput, calls=%fused_computation.16 | convolution fusion | flops 549519360 | bytes 929792 | tf_op jit(solution)/shard_map/dot_general | solution.py:31
  43.0 0.0 collective-permute-done.4
  43.1 1.2 %multiply_reduce_fusion = f32[4096]{0:T(1024)S(1)} fusion(bf16[4096,128]{0,1:T(8,128)(2,1)} %collective-permute-done.4), kind=kLoop, calls=%fused_computation.22 | loop fusion | flops 782336 | bytes 540672 | tf_op jit(solution)/shard_map/reduce_sum | solution.py:19
  44.2 7.5 %fusion.3 = f32[1024,64]{0,1:T(8,128)S(1)} fusion(bf16[1024,64]{0,1:T(8,128)(2,1)S(1)} %get-tuple-element.14, f32[1024]{0:T(1024)S(1)} %get-tuple-element.13, f32[4096]{0:T(1024)S(1)} %multiply_reduce_fusion, bf16[4096,128]{0,1:T(8,128)(2,1)} %collective-permute-done.4), kind=kOutput, calls=%fused_computation.10 | convolution fusion | flops 1098907648 | bytes 1462272 | tf_op jit(solution)/shard_map/dot_general | solution.py:31
  51.7 4.2 %collective-permute-start.6 = (f32[1024,64]{0,1:T(8,128)S(1)}, f32[1024,64]{0,1:T(8,128)S(1)}, u32[]{:S(2)}, u32[]{:S(2)}) collective-permute-start(f32[1024,64]{0,1:T(8,128)S(1)} %fusion.3), channel_id=1, source_target_pairs={{0,256},{64,320},{128,384},{192,448},{256,0},{320,64},{384,128},{4... | collective-permute-start | bytes 786440 | tf_op jit(solution)/shard_map/ppermute | solution.py:15
  55.9 7.3 %fusion.2 = f32[1024,64]{0,1:T(8,128)S(1)} fusion(bf16[1024,64]{0,1:T(8,128)(2,1)S(1)} %collective-permute-done.3, f32[4096]{0:T(1024)S(1)} %multiply_reduce_fusion, f32[1024]{0:T(1024)S(1)} %multiply_reduce_fusion.3, bf16[4096,128]{0,1:T(8,128)(2,1)} %collective-permute-done.4), kind=kOutput, calls=%fused_computation.9 | convolution fusion | flops 1098907648 | bytes 1462272 | tf_op jit(solution)/shard_map/dot_general | solution.py:31
  63.3 3.2 %collective-permute-start.5 = (f32[1024,128]{0,1:T(8,128)S(1)}, f32[1024,128]{0,1:T(8,128)S(1)}, u32[]{:S(2)}, u32[]{:S(2)}) collective-permute-start(f32[1024,128]{0,1:T(8,128)S(1)} %pad_maximum_fusion.2), channel_id=1, source_target_pairs={{0,256},{64,320},{128,384},{192,448},{256,0},{320,64},{384,128},{4... | collective-permute-start | bytes 1572872 | tf_op jit(solution)/shard_map/ppermute | solution.py:15
  66.4 0.4 convolution_bitcast_fusion
  66.8 0.4 fusion.61
  67.2 0.0 collective-permute-done.6
  67.2 0.4 fusion.22
  67.5 13.2 %collective-permute-done.5 = f32[1024,128]{0,1:T(8,128)S(1)} collective-permute-done((f32[1024,128]{0,1:T(8,128)S(1)}, f32[1024,128]{0,1:T(8,128)S(1)}, u32[]{:S(2)}, u32[]{:S(2)}) %collective-permute-start.5) | collective-permute-done | bytes 524320 | tf_op jit(solution)/shard_map/ppermute | solution.py:15
  80.7 0.1 slice_multiply_fusion
  80.8 0.4 convolution_add_fusion
  81.2 0.4 fusion.60
  81.5 2.2 %collective-permute-start.8 = (f32[2,64,64]{2,1,0:T(8,128)S(1)}, f32[2,64,64]{2,1,0:T(8,128)S(1)}, u32[]{:S(2)}, u32[]{:S(2)}) collective-permute-start(f32[2,64,64]{2,1,0:T(8,128)S(1)} %pad_maximum_fusion.5), channel_id=1, source_target_pairs={{0,128},{64,192},{128,0},{192,64},{256,384},{320,448},{384,256},{4... | collective-permute-start | bytes 98312 | tf_op jit(solution)/shard_map/ppermute | solution.py:15
  83.7 3.9 %collective-permute-start.9 = (f32[2,64,64]{2,1,0:T(8,128)S(1)}, f32[2,64,64]{2,1,0:T(8,128)S(1)}, u32[]{:S(2)}, u32[]{:S(2)}) collective-permute-start(f32[2,64,64]{2,1,0:T(8,128)S(1)} %pad_maximum_fusion.5), channel_id=1, source_target_pairs={{0,192},{64,128},{128,64},{192,0},{256,448},{320,384},{384,320},{4... | collective-permute-start | bytes 98312 | tf_op jit(solution)/shard_map/ppermute | solution.py:15
  87.7 3.1 %collective-permute-start.7 = (f32[3,64,64]{2,1,0:T(8,128)S(1)}, f32[3,64,64]{2,1,0:T(8,128)S(1)}, u32[]{:S(2)}, u32[]{:S(2)}) collective-permute-start(f32[3,64,64]{2,1,0:T(8,128)S(1)} %pad_maximum_fusion.4), channel_id=1, source_target_pairs={{0,64},{64,0},{128,192},{192,128},{256,320},{320,256},{384,448},{4... | collective-permute-start | bytes 147464 | tf_op jit(solution)/shard_map/ppermute | solution.py:15
  90.8 0.1 pad_maximum_fusion.1
  90.9 0.0 copy-start.3
  90.9 1.3 %copy.6 = f32[1024,256]{1,0:T(8,128)} copy(f32[1024,256]{0,1:T(8,128)S(1)} %pad_maximum_fusion.1) | data formatting | bytes 2097152
  92.2 0.0 collective-permute-done.8
  92.2 0.0 collective-permute-done.9
  92.2 2.0 %collective-permute-done.7 = f32[3,64,64]{2,1,0:T(8,128)S(1)} collective-permute-done((f32[3,64,64]{2,1,0:T(8,128)S(1)}, f32[3,64,64]{2,1,0:T(8,128)S(1)}, u32[]{:S(2)}, u32[]{:S(2)}) %collective-permute-start.7) | collective-permute-done | bytes 49184 | tf_op jit(solution)/shard_map/ppermute | solution.py:15
  94.2 0.7 maximum_multiply_fusion
  (11 shorter events, 0.2 us)
Async XLA Ops:
  0.6 0.9 copy-start
  0.6 5.8 %copy-start.1 = (bf16[1024,64]{0,1:T(8,128)(2,1)S(1)}, bf16[1024,64]{0,1:T(8,128)(2,1)}, u32[]{:S(2)}) copy-start(bf16[1024,64]{0,1:T(8,128)(2,1)} %param.5) | copy-start | bytes 393220
  3.3 13.6 %collective-permute-start.3 = (bf16[1024,64]{0,1:T(8,128)(2,1)S(1)}, bf16[1024,64]{0,1:T(8,128)(2,1)S(1)}, u32[]{:S(2)}, u32[]{:S(2)}) collective-permute-start(bf16[1024,64]{0,1:T(8,128)(2,1)S(1)} %get-tuple-element.14), channel_id=1, source_target_pairs={{0,256},{64,320},{128,384},{192,448},{256,0},{320,64},{384,128},{4... | collective-permute-start | bytes 393224 | tf_op jit(solution)/shard_map/ppermute | solution.py:15
  6.4 12.9 %collective-permute-start = (bf16[1024,128]{0,1:T(8,128)(2,1)S(1)}, bf16[1024,128]{0,1:T(8,128)(2,1)S(1)}, u32[]{:S(2)}, u32[]{:S(2)}) collective-permute-start(bf16[1024,128]{0,1:T(8,128)(2,1)S(1)} %pad_maximum_fusion.3), channel_id=1, source_target_pairs={{0,64},{64,0},{128,192},{192,128},{256,320},{320,256},{384,448},{4... | collective-permute-start | bytes 786440 | tf_op jit(solution)/shard_map/ppermute | solution.py:15
  9.8 14.2 %collective-permute-start.1 = (bf16[1024,128]{0,1:T(8,128)(2,1)S(1)}, bf16[1024,128]{0,1:T(8,128)(2,1)S(1)}, u32[]{:S(2)}, u32[]{:S(2)}) collective-permute-start(bf16[1024,128]{0,1:T(8,128)(2,1)S(1)} %pad_maximum_fusion.3), channel_id=1, source_target_pairs={{0,128},{64,192},{128,0},{192,64},{256,384},{320,448},{384,256},{4... | collective-permute-start | bytes 786440 | tf_op jit(solution)/shard_map/ppermute | solution.py:15
  14.5 14.8 %collective-permute-start.2 = (bf16[1024,128]{0,1:T(8,128)(2,1)S(1)}, bf16[1024,128]{0,1:T(8,128)(2,1)S(1)}, u32[]{:S(2)}, u32[]{:S(2)}) collective-permute-start(bf16[1024,128]{0,1:T(8,128)(2,1)S(1)} %pad_maximum_fusion.3), channel_id=1, source_target_pairs={{0,192},{64,128},{128,64},{192,0},{256,448},{320,384},{384,320},{4... | collective-permute-start | bytes 786440 | tf_op jit(solution)/shard_map/ppermute | solution.py:15
  29.3 13.7 %collective-permute-start.4 = (bf16[4096,128]{0,1:T(8,128)(2,1)S(1)}, bf16[4096,128]{0,1:T(8,128)(2,1)}, u32[]{:S(2)}, u32[]{:S(2)}) collective-permute-start(bf16[4096,128]{0,1:T(8,128)(2,1)S(1)} %pad_maximum_fusion), channel_id=1, source_target_pairs={{0,1},{1,0},{2,3},{3,2},{4,5},{5,4},{6,7},{7,6},{8,9},{9,8},{10,11... | collective-permute-start | bytes 3145736 | tf_op jit(solution)/shard_map/ppermute | solution.py:15
  31.7 5.4 %copy-start.2 = (f32[1024,64]{0,1:T(8,128)S(1)}, f32[1024,64]{0,1:T(8,128)}, u32[]{:S(2)}) copy-start(f32[1024,64]{0,1:T(8,128)} %fusion.7) | copy-start | bytes 786436
  51.7 15.4 %collective-permute-start.6 = (f32[1024,64]{0,1:T(8,128)S(1)}, f32[1024,64]{0,1:T(8,128)S(1)}, u32[]{:S(2)}, u32[]{:S(2)}) collective-permute-start(f32[1024,64]{0,1:T(8,128)S(1)} %fusion.3), channel_id=1, source_target_pairs={{0,256},{64,320},{128,384},{192,448},{256,0},{320,64},{384,128},{4... | collective-permute-start | bytes 786440 | tf_op jit(solution)/shard_map/ppermute | solution.py:15
  63.3 17.5 %collective-permute-start.5 = (f32[1024,128]{0,1:T(8,128)S(1)}, f32[1024,128]{0,1:T(8,128)S(1)}, u32[]{:S(2)}, u32[]{:S(2)}) collective-permute-start(f32[1024,128]{0,1:T(8,128)S(1)} %pad_maximum_fusion.2), channel_id=1, source_target_pairs={{0,256},{64,320},{128,384},{192,448},{256,0},{320,64},{384,128},{4... | collective-permute-start | bytes 1572872 | tf_op jit(solution)/shard_map/ppermute | solution.py:15
  81.5 10.7 %collective-permute-start.8 = (f32[2,64,64]{2,1,0:T(8,128)S(1)}, f32[2,64,64]{2,1,0:T(8,128)S(1)}, u32[]{:S(2)}, u32[]{:S(2)}) collective-permute-start(f32[2,64,64]{2,1,0:T(8,128)S(1)} %pad_maximum_fusion.5), channel_id=1, source_target_pairs={{0,128},{64,192},{128,0},{192,64},{256,384},{320,448},{384,256},{4... | collective-permute-start | bytes 98312 | tf_op jit(solution)/shard_map/ppermute | solution.py:15
  83.7 8.5 %collective-permute-start.9 = (f32[2,64,64]{2,1,0:T(8,128)S(1)}, f32[2,64,64]{2,1,0:T(8,128)S(1)}, u32[]{:S(2)}, u32[]{:S(2)}) collective-permute-start(f32[2,64,64]{2,1,0:T(8,128)S(1)} %pad_maximum_fusion.5), channel_id=1, source_target_pairs={{0,192},{64,128},{128,64},{192,0},{256,448},{320,384},{384,320},{4... | collective-permute-start | bytes 98312 | tf_op jit(solution)/shard_map/ppermute | solution.py:15
  87.7 6.5 %collective-permute-start.7 = (f32[3,64,64]{2,1,0:T(8,128)S(1)}, f32[3,64,64]{2,1,0:T(8,128)S(1)}, u32[]{:S(2)}, u32[]{:S(2)}) collective-permute-start(f32[3,64,64]{2,1,0:T(8,128)S(1)} %pad_maximum_fusion.4), channel_id=1, source_target_pairs={{0,64},{64,0},{128,192},{192,128},{256,320},{320,256},{384,448},{4... | collective-permute-start | bytes 147464 | tf_op jit(solution)/shard_map/ppermute | solution.py:15
  90.9 3.3 %copy-start.3 = (f32[4]{0:T(128)S(1)}, f32[4]{0:T(128)}, u32[]{:S(2)}) copy-start(f32[4]{0:T(128)} %constant.7) | copy-start | bytes 52
